TPU v7x, 128 devices: a whole 4x4x4 slice. The times are simulated.
128 devices in a mesh: seq: 16 (over x_hi, z, core), tp: 8 (over y, x_lo).
Axes of the slice: x: 4 (x_hi: 2, x_lo: 2; x = x_hi * 2 + x_lo), y: 4, z: 4, core: 2. Of those that a mesh axis runs over, the one named last changes fastest.
Arguments:
- tokens: bfloat16 [4, 2048, 4096], P(None, 'seq', 'tp'), may hold values from -6 to 6
- new_tokens: bfloat16 [4, 4096], P(None, 'tp'), may hold values from -6 to 6
- w_qkv: bfloat16 [3, 4096, 4096], P(None, None, 'tp')
- w_out: bfloat16 [4096, 4096], P('tp')
- q_gain: float32 [4096], P('tp'), may hold values from 0.5 to 6
- k_gain: float32 [4096], P('tp'), may hold values from 0.5 to 6
- post_gain: float32 [4096], P('tp'), may hold values from 0.5 to 1.5
- lengths: int32 [4], replicated, may hold values from 1 to 2048, 6144 in all
Outputs:
- hidden_out: bfloat16 [4, 2048, 4096], P(None, 'seq', 'tp')
- new_out: bfloat16 [4, 4096], P(None, 'tp')
Inputs may be any that keep to these rules, and one draw needn't show every extreme that they name: `lengths`: one prompt has exactly 2048 live tokens.
All inputs are finite; a program needn't handle non-finite values.
Results may differ from a plain program's by a relative error of at most 0.012.
The roundings to bfloat16 on the way count: a program that leaves them out, or rounds other values in their place, can miss the bound.
Values may be sent and summed in bfloat16 or wider, within the bound.
No kernel may reach another device: no remote copies, remote signals or barrier semaphores. Data moves between devices by JAX's collectives and lax.ppermute only.
A program may use at most 128 MiB of HBM per device.

v0:
```python
import jax
import jax.numpy as jnp
from jax import lax
from jax.sharding import PartitionSpec as P

HD = 128
rope_base = 500000.0
norm_eps = 1e-06
masked_fill = -1e30


def rotate(values, position):
    half = values.shape[-1] // 2
    freq = rope_base ** (-(jnp.arange(half, dtype=jnp.float32) * 2.0) / values.shape[-1])
    angle = position.astype(jnp.float32)[..., None] * freq
    cosine = jnp.cos(angle)
    sine = jnp.sin(angle)
    lower = values[..., :half]
    upper = values[..., half:]
    return jnp.concatenate([lower * cosine - upper * sine, upper * cosine + lower * sine], -1)


def attend_pair(q_all, k_all, v_all, q_new, k_new, v_new, length):
    count = q_all.shape[0]
    scale = HD ** (-0.5)
    scores = jnp.dot(q_all, k_all.T, preferred_element_type=jnp.float32) * scale
    query_pos = jnp.arange(count, dtype=jnp.int32)[:, None]
    key_pos = jnp.arange(count, dtype=jnp.int32)[None, :]
    valid = (key_pos <= query_pos) & (key_pos < length)
    scores = jnp.where(valid, scores, masked_fill)
    top = jnp.max(scores, -1, keepdims=True)
    weights = jnp.where(valid, jnp.exp(scores - top), 0.0)
    total = jnp.sum(weights, -1, keepdims=True)
    prompt_out = (
        jnp.dot(weights.astype(jnp.bfloat16), v_all, preferred_element_type=jnp.float32) / total
    ).astype(jnp.bfloat16)
    new_scores = jnp.dot(k_all, q_new, preferred_element_type=jnp.float32) * scale
    live = jnp.arange(count, dtype=jnp.int32) < length
    new_scores = jnp.where(live, new_scores, masked_fill)
    self_score = jnp.dot(q_new, k_new, preferred_element_type=jnp.float32) * scale
    new_top = jnp.maximum(jnp.max(new_scores), self_score)
    new_weights = jnp.where(live, jnp.exp(new_scores - new_top), 0.0)
    own_weight = jnp.exp(self_score - new_top)
    new_total = jnp.sum(new_weights) + own_weight
    own_rounded = lax.optimization_barrier(own_weight.astype(jnp.bfloat16)).astype(jnp.float32)
    numer = jnp.dot(new_weights.astype(jnp.bfloat16), v_all, preferred_element_type=jnp.float32)
    numer = numer + own_rounded * v_new.astype(jnp.float32)
    return (prompt_out, (numer / new_total).astype(jnp.bfloat16))


def body(tokens, new_tokens, w_qkv, w_out, q_gain, k_gain, post_gain, lengths):
    seqs, pos_dev, width_local = tokens.shape
    heads_local = width_local // HD
    full_width = w_qkv.shape[1]
    n_seq = lax.axis_size("seq")
    pairs = seqs * heads_local
    assert pairs == n_seq
    prompt_rows = seqs * pos_dev
    full_len = pos_dev * n_seq
    flat_rows = tokens.reshape(prompt_rows, width_local)
    local_rows = jnp.concatenate([flat_rows, new_tokens], 0)
    all_rows = lax.all_gather(local_rows, "tp", axis=1, tiled=True)
    proj = jnp.einsum("tn,cnf->ctf", all_rows, w_qkv, preferred_element_type=jnp.float32)
    query_raw, key_raw = (proj[0], proj[1])
    query_sq, key_sq = lax.psum(
        (jnp.sum(query_raw * query_raw, -1), jnp.sum(key_raw * key_raw, -1)), "tp"
    )

    def normed(values, square_sum, gain):
        return values * lax.rsqrt(square_sum[:, None] / full_width + norm_eps) * gain

    seq_index = lax.axis_index("seq")
    query_pos = seq_index * pos_dev + jnp.arange(pos_dev, dtype=jnp.int32)
    row_pos = jnp.concatenate([jnp.tile(query_pos, seqs), lengths.astype(jnp.int32)], 0)
    rows_all = prompt_rows + seqs
    queries = rotate(
        normed(query_raw, query_sq, q_gain).reshape(rows_all, heads_local, HD), row_pos[:, None]
    ).astype(jnp.bfloat16)
    keys = rotate(
        normed(key_raw, key_sq, k_gain).reshape(rows_all, heads_local, HD), row_pos[:, None]
    ).astype(jnp.bfloat16)
    values = proj[2].astype(jnp.bfloat16).reshape(rows_all, heads_local, HD)
    qkv = jnp.stack([queries[:prompt_rows], keys[:prompt_rows], values[:prompt_rows]], 0)
    qkv = qkv.reshape(3, seqs, pos_dev, heads_local, HD).transpose(1, 3, 0, 2, 4)
    qkv = qkv.reshape(pairs, 3, pos_dev, HD)
    got = lax.all_to_all(qkv, "seq", 0, 0, tiled=True)
    full = got.transpose(1, 0, 2, 3).reshape(3, full_len, HD)
    owner = seq_index
    own_prompt = owner // heads_local
    new_q = queries[prompt_rows:].reshape(pairs, HD)[owner]
    new_k = keys[prompt_rows:].reshape(pairs, HD)[owner]
    new_v = values[prompt_rows:].reshape(pairs, HD)[owner]
    prompt_out, new_out = attend_pair(
        full[0], full[1], full[2], new_q, new_k, new_v, lengths[own_prompt]
    )
    pad = 8
    back = jnp.concatenate(
        [prompt_out.reshape(n_seq, pos_dev, HD), jnp.broadcast_to(new_out, (n_seq, pad, HD))], 1
    )
    ret = lax.all_to_all(back, "seq", 0, 0, tiled=True)
    ret = ret.reshape(seqs, heads_local, pos_dev + pad, HD)
    attn_rows = ret[:, :, :pos_dev].transpose(0, 2, 1, 3).reshape(prompt_rows, width_local)
    attn_new = ret[:, :, pos_dev].reshape(seqs, width_local)
    attention = jnp.concatenate([attn_rows, attn_new], 0)
    part = jnp.dot(attention, w_out, preferred_element_type=jnp.float32)
    summed = lax.psum_scatter(
        part.astype(jnp.bfloat16), "tp", scatter_dimension=1, tiled=True
    ).astype(jnp.float32)
    square = lax.psum(jnp.sum(summed * summed, -1), "tp")
    out = (
        local_rows.astype(jnp.float32)
        + summed * lax.rsqrt(square[:, None] / full_width + norm_eps) * post_gain
    ).astype(jnp.bfloat16)
    return (out[:prompt_rows].reshape(seqs, pos_dev, width_local), out[prompt_rows:])


def solution(mesh):
    in_specs = (
        P(None, "seq", "tp"),
        P(None, "tp"),
        P(None, None, "tp"),
        P("tp", None),
        P("tp"),
        P("tp"),
        P("tp"),
        P(),
    )
    out_specs = (P(None, "seq", "tp"), P(None, "tp"))
    return jax.shard_map(body, mesh=mesh, in_specs=in_specs, out_specs=out_specs, check_vma=False)
```

profile of v0, /device:TPU:4, one launch (start us, length us, event | category | flops | bytes accessed | tf_op | source)
XLA Modules:
  0.0 334.7 jit_solution(7153203666881482094)
XLA Ops:
  7.2 1.9 pad_maximum_fusion.2
  9.2 1.7 multiply_cosine_fusion
  11.0 92.7 %all-gather.2.cloned.1.call-done = bf16[516,4096]{1,0:T(8,128)(2,1)} async-done(((bf16[516,512]{1,0:T(8,128)(2,1)}), bf16[516,4096]{1,0:T(8,128)(2,1)}) %all-gather.2.cloned.1.call-update) | async-done | bytes 4227088 | tf_op jit(solution)/shard_map/all_gather | solution.py:62
  103.7 10.6 %fusion.45 = (bf16[3,516,512]{2,1,0:T(8,128)(2,1)S(1)}, f32[3,516,512]{2,1,0:T(8,128)S(1)}) fusion(bf16[3,4096,512]{2,1,0:T(8,128)(2,1)} %param.10, bf16[516,4096]{1,0:T(8,128)(2,1)} %all-gather.2.cloned.1.call-done), kind=kOutput, calls=%fused_computation.82 | convolution fusion | flops 6493575168 | bytes 21565440 | tf_op jit(solution)/shard_map/tn,cnf->ctf/dot_general | solution.py:63
  115.7 0.9 copy.12
  117.3 18.3 %all-reduce = (f32[516]{0:T(1024)S(1)}, f32[516]{0:T(1024)S(1)}) all-reduce(f32[516]{0:T(1024)S(1)} %get-tuple-element.3, f32[516]{0:T(1024)S(1)} %get-tuple-element.2), channel_id=1, replica_groups=mesh['seq'=16,'tp'=8] {'tp'}, use_global_device_ids=true, to_apply=%region_3.0 | all-reduce | flops 1032 | bytes 8256 | tf_op jit(solution)/shard_map/psum | solution.py:65
  135.7 1.5 multiply_multiply_fusion.1
  137.2 1.5 multiply_multiply_fusion
  138.8 1.7 add_convert_fusion.1
  142.4 1.3 pad_maximum_fusion
  143.7 7.4 %all-to-all-start = ((bf16[16,3,128,128]{3,2,1,0:T(8,128)(2,1)}), bf16[16,3,128,128]{3,2,1,0:T(8,128)(2,1)S(1)}, u32[]{:S(2)}, u32[]{:S(2)}) async-start(bf16[16,3,128,128]{3,2,1,0:T(8,128)(2,1)} %bitcast.10), calls=%async_computation | async-start | bytes 3145728 | tf_op jit(solution)/shard_map/all_to_all | solution.py:86
  155.4 16.7 %all-to-all-done = bf16[16,3,128,128]{3,2,1,0:T(8,128)(2,1)S(1)} async-done(((bf16[16,3,128,128]{3,2,1,0:T(8,128)(2,1)}), bf16[16,3,128,128]{3,2,1,0:T(8,128)(2,1)S(1)}, u32[]{:S(2)}, u32[]{:S(2)}) %all-to-all-start) | async-done | bytes 1572896 | tf_op jit(solution)/shard_map/all_to_all | solution.py:86
  172.4 1.3 fusion.28
  174.4 1.3 fusion.29
  176.3 5.9 %fusion.1 = (f32[2048]{0:T(1024)S(1)}, f32[2048,2048]{0,1:T(8,128)S(1)}) fusion(pred[2048]{0:T(1024)(128)(4,1)S(1)} %iota_compare_fusion.1, bf16[2048,128]{1,0:T(8,128)(2,1)S(1)} %bitcast.92, bf16[2048,128]{1,0:T(8,128)(2,1)S(1)} %bitcast.88), kind=kOutput, calls=%fused_computation.4 | convolution fusion | flops 1094711296 | bytes 17836032 | tf_op jit(solution)/shard_map/dot_general | solution.py:26
  182.2 8.4 %fusion.6 = f32[2048]{0:T(1024)S(1)} fusion(f32[2048]{0:T(1024)S(1)} %get-tuple-element.23, f32[2048,2048]{0,1:T(8,128)S(1)} %get-tuple-element.24, pred[2048]{0:T(1024)(128)(4,1)S(1)} %iota_compare_fusion.1), kind=kLoop, calls=%fused_computation.10 | loop fusion | flops 29358080 | bytes 16795648 | tf_op jit(solution)/shard_map/reduce_sum | solution.py:33
  190.6 3.5 %fusion.10 = bf16[2048,128]{1,0:T(8,128)(2,1)S(1)} fusion(bf16[2048,128]{1,0:T(8,128)(2,1)S(1)} %bitcast.85, f32[2048]{0:T(1024)S(1)} %get-tuple-element.23, f32[2048,2048]{0,1:T(8,128)S(1)} %get-tuple-element.24, pred[2048]{0:T(1024)(128)(4,1)S(1)} %iota_compare_fusion.1, f32[2048]{0:T(1024)S(1)} %fusion.6), kind=kOutput, calls=%fused_computation.12 | convolution fusion | flops 1103626240 | bytes 17844224 | tf_op jit(solution)/shard_map/dot_general | solution.py:35
  194.4 17.3 %all_to_all.10 = bf16[16,136,128]{2,1,0:T(8,128)(2,1)S(1)} all-to-all(bf16[16,136,128]{2,1,0:T(8,128)(2,1)S(1)} %pad_maximum_fusion.1), channel_id=1, replica_groups=mesh['seq'=16,'tp'=8] {'seq'}, dimensions={0} | all-to-all | bytes 1114112 | tf_op jit(solution)/shard_map/all_to_all | solution.py:100
  212.3 4.4 %convolution_convert_fusion = bf16[516,4096]{1,0:T(8,128)(2,1)} fusion(bf16[512,4096]{1,0:T(8,128)(2,1)S(1)} %copy-done.10, bf16[4,512]{1,0:T(4,128)(2,1)S(1)} %bitcast.98, bf16[512,512]{1,0:T(8,128)(2,1)S(1)} %bitcast.91), kind=kOutput, calls=%fused_computation.7 | convolution fusion | flops 2167431168 | bytes 8949760 | tf_op jit(solution)/shard_map/dot_general | solution.py:105
  216.7 89.1 %reduce-scatter.2.cloned.1.call-done = bf16[516,512]{1,0:T(8,128)(2,1)} async-done(((bf16[516,4096]{1,0:T(8,128)(2,1)}), bf16[516,512]{1,0:T(8,128)(2,1)}) %reduce-scatter.2.cloned.1.call-update) | async-done | bytes 528400 | tf_op jit(solution)/shard_map/reduce_scatter | solution.py:106
  305.8 1.2 fusion.19
  307.0 18.0 %psum.23 = f32[516]{0:T(1024)S(1)} all-reduce(f32[516]{0:T(1024)S(1)} %fusion.19), channel_id=1, replica_groups=mesh['seq'=16,'tp'=8] {'tp'}, use_global_device_ids=true, to_apply=%region_10.11 | all-reduce | flops 516 | bytes 4128 | tf_op jit(solution)/shard_map/psum | solution.py:109
  325.1 1.3 fusion.22
  327.0 0.8 slice.104
  (61 shorter events, 9.4 us)
Async XLA Ops:
  7.2 2.0 copy-start.9
  7.2 96.5 %all-gather.2.cloned.1.call-start = ((), (), s32[]{:S(2)}) async-start(), calls=%async_computation.3 | async-start | bytes 4792320 | tf_op jit(solution)/shard_map/all_gather | solution.py:62
  114.3 1.2 copy-start.4
  116.9 18.8 %copy-start.6 = (f32[512]{0:T(512)S(1)}, f32[512]{0:T(512)}, u32[]{:S(2)}) copy-start(f32[512]{0:T(512)} %param.12) | copy-start | bytes 6148
  117.3 19.9 %copy-start.7 = (f32[512]{0:T(512)S(1)}, f32[512]{0:T(512)}, u32[]{:S(2)}) copy-start(f32[512]{0:T(512)} %param.13) | copy-start | bytes 6148
  137.2 1.6 copy-start.3
  140.5 1.6 copy-start
  141.4 1.0 copy-start.2
  143.7 28.4 %all-to-all-start = ((bf16[16,3,128,128]{3,2,1,0:T(8,128)(2,1)}), bf16[16,3,128,128]{3,2,1,0:T(8,128)(2,1)S(1)}, u32[]{:S(2)}, u32[]{:S(2)}) async-start(bf16[16,3,128,128]{3,2,1,0:T(8,128)(2,1)} %bitcast.10), calls=%async_computation | async-start | bytes 3145728 | tf_op jit(solution)/shard_map/all_to_all | solution.py:86
  151.1 154.7 %reduce-scatter.2.cloned.1.call-start = ((), (), s32[]{:S(2)}) async-start(), calls=%async_computation.4 | async-start | bytes 4792320 | tf_op jit(solution)/shard_map/reduce_scatter | solution.py:106
  194.4 17.9 %copy-start.10 = (bf16[512,4096]{1,0:T(8,128)(2,1)S(1)}, bf16[512,4096]{1,0:T(8,128)(2,1)}, u32[]{:S(2)}) copy-start(bf16[512,4096]{1,0:T(8,128)(2,1)} %param.11) | copy-start | bytes 12582916
  216.6 108.4 %copy-start.1 = (bf16[4,128,512]{2,1,0:T(8,128)(2,1)S(1)}, bf16[4,128,512]{2,1,0:T(8,128)(2,1)}, u32[]{:S(2)}) copy-start(bf16[4,128,512]{2,1,0:T(8,128)(2,1)} %param.8) | copy-start | bytes 1572868
  216.6 108.4 %copy-start.5 = (bf16[4,512]{1,0:T(4,128)(2,1)S(1)}, bf16[4,512]{1,0:T(4,128)(2,1)}, u32[]{:S(2)}) copy-start(bf16[4,512]{1,0:T(4,128)(2,1)} %param.9) | copy-start | bytes 12292
  216.6 108.4 %copy-start.8 = (f32[512]{0:T(512)S(1)}, f32[512]{0:T(512)}, u32[]{:S(2)}) copy-start(f32[512]{0:T(512)} %param.14) | copy-start | bytes 6148
Sparse Core Ops, SparseCore 0:
  9.7 93.9 all-gather.1
  216.8 88.9 reduce-scatter.1
where the time goes:
time: 335 us
  waiting for transfers between devices  199 us (59%)
  blocking collectives  53.6 us (16%)
  other arithmetic  27.2 us (8%)
  matrix products  24.8 us (7%)
  between operations  16.4 us (5%)
  starting transfers between devices  7.66 us (2%)
  local copies, waits for them, and re-layouts  6.41 us (2%)
    all_gather x1, waiting for transfers between devices, body(): all_rows = lax.all_gather(local_rows, 'tp', axis=1, tiled=True)  92.7 us
    reduce_scatter x1, waiting for transfers between devices, body(): lax.psum_scatter(part.astype(jnp.bfloat16), 'tp', scatter_dimension=1, ti...  89.1 us
    psum x1, blocking collectives, body(): lax.psum((jnp.sum(query_raw * query_raw, -1), jnp.sum(key_raw * key_raw,...  18.3 us
    psum x1, blocking collectives, body(): square = lax.psum(jnp.sum(summed * summed, -1), 'tp')  18 us
    all_to_all x1, blocking collectives, body(): ret = lax.all_to_all(back, 'seq', 0, 0, tiled=True)  17.3 us
    all_to_all x1, waiting for transfers between devices, body(): got = lax.all_to_all(qkv, 'seq', 0, 0, tiled=True)  16.7 us
    dot_general x1, matrix products, body(): jnp.einsum('tn,cnf->ctf', all_rows, w_qkv, preferred_element_type=jnp.flo...  10.6 us
    reduce_sum x1, other arithmetic, attend_pair(): total = jnp.sum(weights, -1, keepdims=True)  8.42 us
  transfers between devices with their start and end apart: 3, of which 3 were waited for; matrix products, arithmetic and copies ran while one was open for 2% of the time, Pallas kernels for 0%

commit v1 on v0

--- a/solution.py
+++ b/solution.py
@@ -59,7 +59,9 @@
     full_len = pos_dev * n_seq
     flat_rows = tokens.reshape(prompt_rows, width_local)
     local_rows = jnp.concatenate([flat_rows, new_tokens], 0)
-    all_rows = lax.all_gather(local_rows, "tp", axis=1, tiled=True)
+    all_rows = jnp.concatenate(
+        lax.all_to_all(jnp.stack([local_rows] * lax.axis_size("tp")), "tp", 0, 0), axis=1
+    )
     proj = jnp.einsum("tn,cnf->ctf", all_rows, w_qkv, preferred_element_type=jnp.float32)
     query_raw, key_raw = (proj[0], proj[1])
     query_sq, key_sq = lax.psum(

time: 335 us -> 311 us (0.928)
  waiting for transfers between devices: 199 us -> 154 us
  local copies, waits for them, and re-layouts: 6.41 us -> 21.8 us
  starting transfers between devices: 7.66 us -> 13.8 us
    all_gather x1 -> x0, waiting for transfers between devices: 92.7 us -> none  [body(): all_rows = lax.all_gather(local_rows, 'tp', axis=1, tiled=True)]
    all_to_all x0 -> x1, waiting for transfers between devices: none -> 48.5 us  [body(): lax.all_to_all(jnp.stack([local_rows] * lax.axis_size('tp')), 'tp', 0, 0)]
    reshape x0 -> x2, local copies, waits for them, and re-layouts: none -> 13.1 us  [body(): jnp.concatenate(lax.all_to_all(jnp.stack([local_rows] * lax.axis_size('tp...]
    all_to_all x0 -> x1, starting transfers between devices: none -> 5.24 us  [body(): lax.all_to_all(jnp.stack([local_rows] * lax.axis_size('tp')), 'tp', 0, 0)]
where the time goes in v1:
time: 311 us
  waiting for transfers between devices  154 us (50%)
  blocking collectives  53.1 us (17%)
  other arithmetic  26.4 us (8%)
  matrix products  24.8 us (8%)
  local copies, waits for them, and re-layouts  21.8 us (7%)
  between operations  16.4 us (5%)
  starting transfers between devices  13.8 us (4%)
    reduce_scatter x1, waiting for transfers between devices, body(): lax.psum_scatter(part.astype(jnp.bfloat16), 'tp', scatter_dimension=1, ti...  89.1 us
    all_to_all x1, waiting for transfers between devices, body(): lax.all_to_all(jnp.stack([local_rows] * lax.axis_size('tp')), 'tp', 0, 0)  48.5 us
    psum x1, blocking collectives, body(): square = lax.psum(jnp.sum(summed * summed, -1), 'tp')  18 us
    psum x1, blocking collectives, body(): lax.psum((jnp.sum(query_raw * query_raw, -1), jnp.sum(key_raw * key_raw,...  17.8 us
    all_to_all x1, blocking collectives, body(): ret = lax.all_to_all(back, 'seq', 0, 0, tiled=True)  17.3 us
    all_to_all x1, waiting for transfers between devices, body(): got = lax.all_to_all(qkv, 'seq', 0, 0, tiled=True)  16.7 us
    reshape x2, local copies, waits for them, and re-layouts, body(): jnp.concatenate(lax.all_to_all(jnp.stack([local_rows] * lax.axis_size('tp...  13.1 us
    dot_general x1, matrix products, body(): jnp.einsum('tn,cnf->ctf', all_rows, w_qkv, preferred_element_type=jnp.flo...  10.6 us
  transfers between devices with their start and end apart: 3, of which 3 were waited for; matrix products, arithmetic and copies ran while one was open for 2% of the time, Pallas kernels for 0%

profile of v1, /device:TPU:4, one launch (start us, length us, event | category | flops | bytes accessed | tf_op | source)
XLA Modules:
  0.0 310.5 jit_solution(703426474194866904)
XLA Ops:
  8.3 2.3 stack.10
  10.5 5.2 %all-to-all-start = ((bf16[8,516,512]{2,1,0:T(8,128)(2,1)}), bf16[8,516,512]{2,1,0:T(8,128)(2,1)}, u32[]{:S(2)}, u32[]{:S(2)}) async-start(bf16[8,516,512]{2,1,0:T(8,128)(2,1)} %stack.10), calls=%async_computation | async-start | bytes 8519680 | tf_op jit(solution)/shard_map/all_to_all | solution.py:63
  15.8 1.7 multiply_cosine_fusion
  17.6 48.5 %all-to-all-done = bf16[8,516,512]{2,1,0:T(8,128)(2,1)} async-done(((bf16[8,516,512]{2,1,0:T(8,128)(2,1)}), bf16[8,516,512]{2,1,0:T(8,128)(2,1)}, u32[]{:S(2)}, u32[]{:S(2)}) %all-to-all-start) | async-done | bytes 4227104 | tf_op jit(solution)/shard_map/all_to_all | solution.py:63
  66.0 5.6 %copy.15 = bf16[516,8,512]{2,1,0:T(8,128)(2,1)} copy(bf16[516,8,512]{2,0,1:T(8,128)(2,1)} %bitcast.2) | data formatting | bytes 8454144 | tf_op jit(solution)/shard_map/reshape | solution.py:62
  71.7 7.5 %reshape.215 = bf16[516,4096,1]{1,0,2:T(8,128)(2,1)} reshape(bf16[516,8,512]{2,1,0:T(8,128)(2,1)} %copy.15) | data formatting | bytes 8454144 | tf_op jit(solution)/shard_map/reshape | solution.py:62
  79.2 10.6 %fusion.40 = (bf16[3,516,512]{2,1,0:T(8,128)(2,1)S(1)}, f32[3,516,512]{2,1,0:T(8,128)S(1)}) fusion(bf16[516,4096,1]{1,0,2:T(8,128)(2,1)} %reshape.215, bf16[3,4096,512]{2,1,0:T(8,128)(2,1)} %param.10), kind=kOutput, calls=%fused_computation.80 | convolution fusion | flops 6493575168 | bytes 21565440 | tf_op jit(solution)/shard_map/tn,cnf->ctf/dot_general | solution.py:65
  92.8 17.8 %all-reduce = (f32[516]{0:T(1024)S(1)}, f32[516]{0:T(1024)S(1)}) all-reduce(f32[516]{0:T(1024)S(1)} %get-tuple-element.3, f32[516]{0:T(1024)S(1)} %get-tuple-element.2), channel_id=1, replica_groups=mesh['seq'=16,'tp'=8] {'tp'}, use_global_device_ids=true, to_apply=%region_3.0 | all-reduce | flops 1032 | bytes 8256 | tf_op jit(solution)/shard_map/psum | solution.py:67
  110.7 1.5 multiply_multiply_fusion.1
  112.2 1.5 multiply_multiply_fusion
  113.8 1.7 add_convert_fusion.1
  117.4 1.3 pad_maximum_fusion
  118.7 8.3 %all-to-all-start.1 = ((bf16[16,3,128,128]{3,2,1,0:T(8,128)(2,1)}), bf16[16,3,128,128]{3,2,1,0:T(8,128)(2,1)S(1)}, u32[]{:S(2)}, u32[]{:S(2)}) async-start(bf16[16,3,128,128]{3,2,1,0:T(8,128)(2,1)} %bitcast.10), calls=%async_computation.1 | async-start | bytes 3145728 | tf_op jit(solution)/shard_map/all_to_all | solution.py:88
  131.3 16.7 %all-to-all-done.1 = bf16[16,3,128,128]{3,2,1,0:T(8,128)(2,1)S(1)} async-done(((bf16[16,3,128,128]{3,2,1,0:T(8,128)(2,1)}), bf16[16,3,128,128]{3,2,1,0:T(8,128)(2,1)S(1)}, u32[]{:S(2)}, u32[]{:S(2)}) %all-to-all-start.1) | async-done | bytes 1572896 | tf_op jit(solution)/shard_map/all_to_all | solution.py:88
  148.3 1.3 fusion.23
  150.2 1.3 fusion.24
  152.2 5.9 %fusion.1 = (f32[2048]{0:T(1024)S(1)}, f32[2048,2048]{0,1:T(8,128)S(1)}) fusion(pred[2048]{0:T(1024)(128)(4,1)S(1)} %iota_compare_fusion.1, bf16[2048,128]{1,0:T(8,128)(2,1)S(1)} %bitcast.87, bf16[2048,128]{1,0:T(8,128)(2,1)S(1)} %bitcast.83), kind=kOutput, calls=%fused_computation.4 | convolution fusion | flops 1094711296 | bytes 17836032 | tf_op jit(solution)/shard_map/dot_general | solution.py:26
  158.1 8.4 %fusion.4 = f32[2048]{0:T(1024)S(1)} fusion(f32[2048]{0:T(1024)S(1)} %get-tuple-element.23, f32[2048,2048]{0,1:T(8,128)S(1)} %get-tuple-element.24, pred[2048]{0:T(1024)(128)(4,1)S(1)} %iota_compare_fusion.1), kind=kLoop, calls=%fused_computation.8 | loop fusion | flops 29358080 | bytes 16795648 | tf_op jit(solution)/shard_map/reduce_sum | solution.py:33
  166.5 3.5 %fusion.8 = bf16[2048,128]{1,0:T(8,128)(2,1)S(1)} fusion(bf16[2048,128]{1,0:T(8,128)(2,1)S(1)} %bitcast.80, f32[2048]{0:T(1024)S(1)} %get-tuple-element.23, f32[2048,2048]{0,1:T(8,128)S(1)} %get-tuple-element.24, pred[2048]{0:T(1024)(128)(4,1)S(1)} %iota_compare_fusion.1, f32[2048]{0:T(1024)S(1)} %fusion.4), kind=kOutput, calls=%fused_computation.10 | convolution fusion | flops 1103626240 | bytes 17844224 | tf_op jit(solution)/shard_map/dot_general | solution.py:35
  170.3 17.3 %all_to_all.15 = bf16[16,136,128]{2,1,0:T(8,128)(2,1)S(1)} all-to-all(bf16[16,136,128]{2,1,0:T(8,128)(2,1)S(1)} %pad_maximum_fusion.1), channel_id=1, replica_groups=mesh['seq'=16,'tp'=8] {'seq'}, dimensions={0} | all-to-all | bytes 1114112 | tf_op jit(solution)/shard_map/all_to_all | solution.py:102
  188.1 4.4 %convolution_convert_fusion = bf16[516,4096]{1,0:T(8,128)(2,1)} fusion(bf16[512,4096]{1,0:T(8,128)(2,1)S(1)} %copy-done.10, bf16[4,512]{1,0:T(4,128)(2,1)S(1)} %bitcast.93, bf16[512,512]{1,0:T(8,128)(2,1)S(1)} %bitcast.86), kind=kOutput, calls=%fused_computation.7 | convolution fusion | flops 2167431168 | bytes 8949760 | tf_op jit(solution)/shard_map/dot_general | solution.py:107
  192.5 89.1 %reduce-scatter.2.cloned.1.call-done = bf16[516,512]{1,0:T(8,128)(2,1)} async-done(((bf16[516,4096]{1,0:T(8,128)(2,1)}), bf16[516,512]{1,0:T(8,128)(2,1)}) %reduce-scatter.2.cloned.1.call-update) | async-done | bytes 528400 | tf_op jit(solution)/shard_map/reduce_scatter | solution.py:108
  282.9 18.0 %psum.23 = f32[516]{0:T(1024)S(1)} all-reduce(f32[516]{0:T(1024)S(1)} %fusion.14), channel_id=1, replica_groups=mesh['seq'=16,'tp'=8] {'tp'}, use_global_device_ids=true, to_apply=%region_10.11 | all-reduce | flops 516 | bytes 4128 | tf_op jit(solution)/shard_map/psum | solution.py:111
  301.0 1.3 fusion.17
  (63 shorter events, 13.4 us)
Async XLA Ops:
  10.5 5.3 %copy-start.9 = (s32[4]{0:T(128)S(1)}, s32[4]{0:T(128)}, u32[]{:S(2)}) copy-start(s32[4]{0:T(128)} %param.15) | copy-start | bytes 52
  10.5 55.5 %all-to-all-start = ((bf16[8,516,512]{2,1,0:T(8,128)(2,1)}), bf16[8,516,512]{2,1,0:T(8,128)(2,1)}, u32[]{:S(2)}, u32[]{:S(2)}) async-start(bf16[8,516,512]{2,1,0:T(8,128)(2,1)} %stack.10), calls=%async_computation | async-start | bytes 8519680 | tf_op jit(solution)/shard_map/all_to_all | solution.py:63
  89.8 1.2 copy-start.4
  92.4 18.2 %copy-start.6 = (f32[512]{0:T(512)S(1)}, f32[512]{0:T(512)}, u32[]{:S(2)}) copy-start(f32[512]{0:T(512)} %param.12) | copy-start | bytes 6148
  92.8 19.4 %copy-start.7 = (f32[512]{0:T(512)S(1)}, f32[512]{0:T(512)}, u32[]{:S(2)}) copy-start(f32[512]{0:T(512)} %param.13) | copy-start | bytes 6148
  112.2 1.6 copy-start.3
  115.5 1.6 copy-start
  116.3 1.0 copy-start.2
  118.7 29.3 %all-to-all-start.1 = ((bf16[16,3,128,128]{3,2,1,0:T(8,128)(2,1)}), bf16[16,3,128,128]{3,2,1,0:T(8,128)(2,1)S(1)}, u32[]{:S(2)}, u32[]{:S(2)}) async-start(bf16[16,3,128,128]{3,2,1,0:T(8,128)(2,1)} %bitcast.10), calls=%async_computation.1 | async-start | bytes 3145728 | tf_op jit(solution)/shard_map/all_to_all | solution.py:88
  127.0 154.7 %reduce-scatter.2.cloned.1.call-start = ((), (), s32[]{:S(2)}) async-start(), calls=%async_computation.4 | async-start | bytes 4792320 | tf_op jit(solution)/shard_map/reduce_scatter | solution.py:108
  170.3 17.9 %copy-start.10 = (bf16[512,4096]{1,0:T(8,128)(2,1)S(1)}, bf16[512,4096]{1,0:T(8,128)(2,1)}, u32[]{:S(2)}) copy-start(bf16[512,4096]{1,0:T(8,128)(2,1)} %param.11) | copy-start | bytes 12582916
  192.5 108.4 %copy-start.1 = (bf16[4,128,512]{2,1,0:T(8,128)(2,1)S(1)}, bf16[4,128,512]{2,1,0:T(8,128)(2,1)}, u32[]{:S(2)}) copy-start(bf16[4,128,512]{2,1,0:T(8,128)(2,1)} %param.8) | copy-start | bytes 1572868
  192.5 108.4 %copy-start.5 = (bf16[4,512]{1,0:T(4,128)(2,1)S(1)}, bf16[4,512]{1,0:T(4,128)(2,1)}, u32[]{:S(2)}) copy-start(bf16[4,512]{1,0:T(4,128)(2,1)} %param.9) | copy-start | bytes 12292
  192.5 108.5 %copy-start.8 = (f32[512]{0:T(512)S(1)}, f32[512]{0:T(512)}, u32[]{:S(2)}) copy-start(f32[512]{0:T(512)} %param.14) | copy-start | bytes 6148
Sparse Core Ops, SparseCore 0:
  192.7 88.9 reduce-scatter.1
